TPU v7x, 32 devices: a whole 2x2x4 slice. The times are simulated.
32 devices in a mesh: section: 2 (over x), mp: 4 (over z), dp: 4 (over y, core).
Axes of the slice: x: 2, y: 2, z: 4, core: 2. Of those that a mesh axis runs over, the one named last changes fastest.
Arguments:
- text_in: bfloat16 [4, 2, 512, 8192], P('dp', 'section', None, 'mp'), may hold values from -6 to 6
- vision: bfloat16 [4, 2, 256, 8192], P('dp', 'section', None, 'mp'), may hold values from -6 to 6
- tile_counts: int32 [4, 2], P('dp'), may hold values from 1 to 4, as said below
- lengths: int32 [4, 2], P('dp', 'section'), may hold values from 128 to 512, as said below
- image_of: int32 [4, 2], P('dp'), may hold values from 0 to 1, each once within a row
- norm_gain: float32 [2, 8192], P('section'), may hold values from 0.5 to 1.5
- query_weight: bfloat16 [2, 8192, 4096], P('section', 'dp', 'mp'), may hold values from -0.0625 to 0.0625
- key_weight: bfloat16 [2, 8192, 1024], P('section', 'dp', 'mp'), may hold values from -0.0625 to 0.0625
- value_weight: bfloat16 [2, 8192, 1024], P('section', 'dp', 'mp'), may hold values from -0.0625 to 0.0625
- query_gain: float32 [2, 128], P('section')
- key_gain: float32 [2, 128], P('section')
- cross_gate: float32 [2], P('section'), may hold values from 0.4 to 1.5
- context_grad: bfloat16 [4, 2, 512, 4096], P('dp', 'section', None, 'mp'), may hold values from -6 to 6
Outputs:
- gated_context: bfloat16 [4, 2, 512, 4096], P('dp', 'section', None, 'mp')
- vision_grad: bfloat16 [4, 2, 256, 8192], P('dp', 'section', None, 'mp')
- key_weight_grad: bfloat16 [2, 8192, 1024], P('section', 'dp', 'mp')
- value_weight_grad: bfloat16 [2, 8192, 1024], P('section', 'dp', 'mp')
Inputs may be any that keep to these rules, and one draw needn't show every extreme that they name: `tile_counts`: some image has 4 tiles and some has one. `lengths`: some sample has the full 512 tokens. `image_of`: each row is a permutation of the sections.
All inputs are finite; a program needn't handle non-finite values.
Results may differ from a plain program's by a relative error of at most 0.018.
Values may be sent and summed in bfloat16 or wider, within the bound.
No kernel may reach another device: no remote copies, remote signals or barrier semaphores. Data moves between devices by JAX's collectives and lax.ppermute only.
A program may use at most 192 MiB of HBM per device.

v0:
```python
import jax
import jax.numpy as jnp
from jax import lax
from jax.sharding import PartitionSpec as P

HD = 128
TILE_ROWS = 64


def shifted(value, axis, steps):
    count = lax.axis_size(axis)
    pairs = [(source, (source + steps) % count) for source in range(count)]
    return lax.ppermute(value, axis, pairs)


def norm_rows(values, gain):
    values = values.astype(jnp.float32)
    scaled = values * lax.rsqrt(jnp.mean(values * values, axis=-1, keepdims=True) + 1e-05)
    return scaled * gain


def rounded(values):
    return lax.optimization_barrier(values.astype(jnp.bfloat16)).astype(jnp.float32)


def attend(queries, keys_raw, values_raw, key_norm, usable, present, gate_value):
    keys = rounded(norm_rows(keys_raw, key_norm))
    values = rounded(values_raw)
    text_rows, heads, depth = queries.shape
    groups = keys.shape[1]
    grouped = queries.astype(jnp.float32).reshape(text_rows, groups, heads // groups, depth)
    scores = jnp.einsum("tgjd,vgd->gjtv", grouped, keys) * depth ** (-0.5)
    scores = jnp.where(usable[None, None, None, :], scores, -1e30)
    highest = lax.stop_gradient(jnp.max(scores, axis=-1, keepdims=True))
    weights = jnp.exp(scores - highest)
    probs = rounded(weights / jnp.sum(weights, axis=-1, keepdims=True))
    context = jnp.einsum("gjtv,vgd->tgjd", probs, values).reshape(text_rows, heads * depth)
    return jnp.where(present[:, None], jnp.tanh(gate_value) * context, 0.0)


def per_device(
    text_in,
    vision,
    tile_counts,
    lengths,
    image_of,
    norm_gain,
    query_weight,
    key_weight,
    value_weight,
    query_gain,
    key_gain,
    cross_gate,
    context_grad,
):
    arrived = shifted(text_in, "section", 1)
    full_text = lax.all_gather(arrived, "mp", axis=3, tiled=True)[0, 0]
    text_rows = full_text.shape[0]
    normed = norm_rows(full_text, norm_gain[0]).astype(jnp.bfloat16)
    width_q = query_weight.shape[2]
    columns = normed
    query_raw = jnp.dot(
        columns,
        lax.all_gather(query_weight, "dp", axis=1, tiled=True)[0],
        preferred_element_type=jnp.float32,
    )
    queries = norm_rows(query_raw.reshape(text_rows, width_q // HD, HD), query_gain[0]).astype(
        jnp.bfloat16
    )
    key_full, value_full = (
        lax.all_gather(key_weight, "dp", axis=1, tiled=True),
        lax.all_gather(value_weight, "dp", axis=1, tiled=True),
    )
    key_full = key_full[0]
    value_full = value_full[0]
    slot_rows = vision.shape[2]
    part_width = vision.shape[3]
    wanted = image_of[0, lax.axis_index("section")]
    shard_piece = lax.all_gather(vision, "section", axis=1, tiled=True)
    owners = jnp.arange(shard_piece.shape[1])
    chosen = (owners == wanted)[:, None, None]
    taken = jnp.where(chosen, shard_piece[0], jnp.zeros_like(shard_piece[0]))
    image_part = jnp.sum(taken.astype(jnp.float32), axis=0).astype(jnp.bfloat16)
    image = lax.all_gather(image_part, "mp", axis=1, tiled=True)
    width_k = key_full.shape[1]
    keys_raw = jnp.dot(image, key_full, preferred_element_type=jnp.float32).reshape(
        slot_rows, width_k // HD, HD
    )
    values_raw = jnp.dot(image, value_full, preferred_element_type=jnp.float32).reshape(
        slot_rows, width_k // HD, HD
    )
    usable = jnp.arange(slot_rows) < tile_counts[0, wanted] * TILE_ROWS
    present = jnp.arange(text_rows) < lengths[0, 0]

    def forward(keys_in, values_in):
        return attend(queries, keys_in, values_in, key_gain[0], usable, present, cross_gate[0])

    context, pullback = jax.vjp(forward, keys_raw, values_raw)
    gated_context = context.astype(jnp.bfloat16).reshape(1, 1, text_rows, width_q)
    key_back, value_back = pullback(context_grad[0, 0].astype(jnp.float32))
    key_flat = key_back.reshape(slot_rows, width_k).astype(jnp.bfloat16)
    value_flat = value_back.reshape(slot_rows, width_k).astype(jnp.bfloat16)
    contract = (((1,), (1,)), ((), ()))
    partial_sum = lax.dot_general(key_flat, key_full, contract, preferred_element_type=jnp.float32)
    partial_sum = partial_sum + lax.dot_general(
        value_flat, value_full, contract, preferred_element_type=jnp.float32
    )
    partial_bf = partial_sum.astype(jnp.bfloat16)
    summed = lax.psum_scatter(
        partial_bf.astype(jnp.float32).astype(jnp.bfloat16), "mp", scatter_dimension=1, tiled=True
    )
    row_ids = jnp.arange(slot_rows * lax.axis_size("section"))
    taken = jnp.take(summed, row_ids % slot_rows, axis=0).astype(jnp.float32)
    routed = lax.psum_scatter(
        jnp.where((row_ids // slot_rows == wanted)[:, None], taken, 0.0).astype(jnp.bfloat16),
        "section",
        scatter_dimension=0,
        tiled=True,
    )
    vision_grad = routed.reshape(1, 1, slot_rows, part_width)
    columns = image
    inner = (((0,), (0,)), ((), ()))
    key_part = lax.dot_general(columns, key_flat, inner, preferred_element_type=jnp.float32).astype(
        jnp.bfloat16
    )
    value_part = lax.dot_general(
        columns, value_flat, inner, preferred_element_type=jnp.float32
    ).astype(jnp.bfloat16)
    both_grads = lax.psum_scatter(
        jnp.concatenate([key_part, value_part], axis=1).astype(jnp.float32).astype(jnp.bfloat16),
        "dp",
        scatter_dimension=0,
        tiled=True,
    )
    key_weight_grad = both_grads[:, :width_k][None]
    value_weight_grad = both_grads[:, width_k:][None]
    return (gated_context, vision_grad, key_weight_grad, value_weight_grad)


def solution(mesh):
    return jax.shard_map(
        per_device,
        mesh=mesh,
        in_specs=(
            P("dp", "section", None, "mp"),
            P("dp", "section", None, "mp"),
            P("dp", None),
            P("dp", "section"),
            P("dp", None),
            P("section", None),
            P("section", "dp", "mp"),
            P("section", "dp", "mp"),
            P("section", "dp", "mp"),
            P("section", None),
            P("section", None),
            P("section"),
            P("dp", "section", None, "mp"),
        ),
        out_specs=(
            P("dp", "section", None, "mp"),
            P("dp", "section", None, "mp"),
            P("section", "dp", "mp"),
            P("section", "dp", "mp"),
        ),
        check_vma=False,
    )
```

profile of v0, /device:TPU:0, one launch (start us, length us, event | category | flops | bytes accessed | tf_op | source)
XLA Modules:
  0.0 705.0 jit_solution(10474390815657424555)
XLA Ops:
  7.2 0.7 all-gather.7.cloned.1.call-update
  7.9 0.0 all-gather.13.cloned.1.call-start
  8.0 0.7 all-gather.13.cloned.1.call-update
  8.7 0.0 all-gather.11.cloned.1.call-start
  8.7 0.7 all-gather.11.cloned.1.call-update
  9.4 0.0 all-gather.9.cloned.1.call-start
  9.5 0.6 constant_dynamic-slice_fusion.1
  10.0 0.6 iota_compare_fusion.2
  10.7 34.7 %all-gather.7.cloned.1.call-done = bf16[1,2,256,2048]{3,2,0,1:T(8,128)(2,1)} async-done(((bf16[1,1,256,2048]{3,2,0,1:T(8,128)(2,1)}), bf16[1,2,256,2048]{3,2,0,1:T(8,128)(2,1)}) %all-gather.7.cloned.1.call-update) | async-done | bytes 2097168 | tf_op jit(solution)/shard_map/all_gather | solution.py:79
  45.4 3.4 fusion.34
  48.8 0.0 all-gather.15.cloned.1.call-start
  48.9 0.4 collective-permute-start
  49.3 47.3 %collective-permute-done = bf16[1,1,512,2048]{3,2,1,0:T(8,128)(2,1)S(1)} collective-permute-done((bf16[1,1,512,2048]{3,2,1,0:T(8,128)(2,1)}, bf16[1,1,512,2048]{3,2,1,0:T(8,128)(2,1)S(1)}, u32[]{:S(2)}, u32[]{:S(2)}) %collective-permute-start) | collective-permute-done | bytes 2097184 | tf_op jit(solution)/shard_map/ppermute | solution.py:13
  96.5 1.4 copy-done.11
  98.0 0.0 all-gather.17.cloned.1.call-start
  98.0 0.5 all-gather.17.cloned.1.call-update
  98.5 0.0 reduce-scatter.4.cloned.1.call-start
  99.9 0.5 copy.81
  102.4 0.6 fusion.100
  103.0 1.2 iota_compare_fusion.1
  104.2 6.4 copy.51
  110.6 7.0 all-gather.11.cloned.1.call-done
  117.6 6.4 copy.50
  123.9 76.4 %all-gather.9.cloned.1.call-done = bf16[256,8192]{1,0:T(8,128)(2,1)} async-done(((bf16[256,2048]{1,0:T(8,128)(2,1)}), bf16[256,8192]{1,0:T(8,128)(2,1)}) %all-gather.9.cloned.1.call-update) | async-done | bytes 4194320 | tf_op jit(solution)/shard_map/all_gather | solution.py:84
  200.4 4.9 multiply_reduce_fusion.2
  205.3 0.7 multiply_convert_fusion.1
  206.0 0.3 copy-done.10
  206.3 1.3 fusion.60
  207.6 2.0 fusion.43
  209.6 140.3 %all-gather.15.cloned.1.call-done = bf16[1,1,512,8192]{3,2,1,0:T(8,128)(2,1)} async-done(((bf16[1,1,512,2048]{3,2,1,0:T(8,128)(2,1)}), bf16[1,1,512,8192]{3,2,1,0:T(8,128)(2,1)}) %all-gather.15.cloned.1.call-update) | async-done | bytes 8388624 | tf_op jit(solution)/shard_map/all_gather | solution.py:57
  350.0 5.1 fusion.1
  355.1 100.4 %all-gather.17.cloned.1.call-done = bf16[1,8192,1024]{2,1,0:T(8,128)(2,1)} async-done(((bf16[1,2048,1024]{2,1,0:T(8,128)(2,1)}), bf16[1,8192,1024]{2,1,0:T(8,128)(2,1)}) %all-gather.17.cloned.1.call-update) | async-done | bytes 16777232 | tf_op jit(solution)/shard_map/all_gather | solution.py:64
  455.5 21.4 %copy.52 = bf16[1024,8192]{1,0:T(8,128)(2,1)} copy(bf16[1024,8192]{0,1:T(8,128)(2,1)} %bitcast.150) | data formatting | bytes 33554432 | tf_op jit(solution)/shard_map/dot_general | solution.py:62
  477.0 14.8 %multiply_reduce_fusion = (f32[512,8]{0,1:T(8,128)S(1)}, f32[512,8,128]{0,2,1:T(8,128)S(1)}) fusion(bf16[8,128,8192]{2,1,0:T(8,128)(2,1)} %bitcast.151, bf16[1,1,512,8192]{3,2,1,0:T(8,128)(2,1)} %all-gather.15.cloned.1.call-done, f32[8192]{0:T(1024)S(1)} %bitcast.169, f32[512]{0:T(512)S(1)} %add_rsqrt_fusion.1), kind=kOutput, calls=%fused_computation.55 | convolution fusion | flops 8607756288 | bytes 27314176 | tf_op jit(solution)/shard_map/dot_general | solution.py:62
  491.8 0.5 multiply_convert_fusion
  492.3 5.1 fusion.101
  497.4 0.7 multiply_divide_fusion
  498.1 3.9 fusion.16
  502.0 0.7 copy-done.9
  502.8 1.2 fusion.66
  504.0 0.1 multiply_reduce_fusion.1
  504.1 0.1 fusion.75
  504.3 0.8 fusion.63
  505.1 1.1 copy-done.4
  506.2 1.3 fusion.19
  507.5 0.9 copy-done.7
  508.4 3.4 fusion.4
  511.8 0.0 reduce-scatter.8.cloned.1.call-start
  511.9 5.5 convolution_convert_fusion
  517.4 3.2 convolution_convert_fusion.1
  520.6 7.7 %pad_maximum_fusion = bf16[8192,512]{0,1:T(8,128)(2,1)} fusion(bf16[8192,256]{0,1:T(8,128)(2,1)} %convolution_convert_fusion, bf16[8192,256]{0,1:T(8,128)(2,1)} %convolution_convert_fusion.1), kind=kLoop, calls=%fused_computation.13 | loop fusion | flops 16777216 | bytes 16777216 | tf_op jit(solution)/shard_map/concatenate | solution.py:130
  528.3 0.0 reduce-scatter.6.cloned.1.call-start
  528.4 0.7 fusion.89
  529.1 59.6 %reduce-scatter.4.cloned.1.call-done = bf16[256,2048]{1,0:T(8,128)(2,1)} async-done(((bf16[256,8192]{1,0:T(8,128)(2,1)}), bf16[256,2048]{1,0:T(8,128)(2,1)}) %reduce-scatter.4.cloned.1.call-update) | async-done | bytes 1048592 | tf_op jit(solution)/shard_map/reduce_scatter | solution.py:109
  588.7 6.8 gather_fusion
  595.5 3.7 select_convert_fusion
  599.3 0.5 convolution_multiply_fusion
  599.8 0.5 copy.57
  600.3 1.2 select_convert_fusion.1
  601.6 62.2 %reduce-scatter.8.cloned.1.call-done = bf16[2048,512]{0,1:T(8,128)(2,1)} async-done(((bf16[8192,512]{0,1:T(8,128)(2,1)}), bf16[2048,512]{0,1:T(8,128)(2,1)}) %reduce-scatter.8.cloned.1.call-update) | async-done | bytes 2097168 | tf_op jit(solution)/shard_map/reduce_scatter | solution.py:129
  663.8 1.7 slice_bitcast_fusion
  665.4 1.3 copy.64
  666.7 1.3 copy.65
  668.0 30.4 %reduce-scatter.6.cloned.1.call-done = bf16[256,2048]{1,0:T(8,128)(2,1)} async-done(((bf16[512,2048]{1,0:T(8,128)(2,1)}), bf16[256,2048]{1,0:T(8,128)(2,1)}) %reduce-scatter.6.cloned.1.call-update) | async-done | bytes 1048592 | tf_op jit(solution)/shard_map/reduce_scatter | solution.py:114
  (49 shorter events, 0.3 us)
Async XLA Ops:
  7.2 2.3 copy-start
  7.2 38.2 %all-gather.7.cloned.1.call-start = ((), (), s32[]{:S(2)}) async-start(), calls=%async_computation.3 | async-start | bytes 3145728 | tf_op jit(solution)/shard_map/all_gather | solution.py:79
  7.9 96.3 %all-gather.13.cloned.1.call-start = ((), (), s32[]{:S(2)}) async-start(), calls=%async_computation.6 | async-start | bytes 5242880 | tf_op jit(solution)/shard_map/all_gather | solution.py:71
  8.7 108.9 %all-gather.11.cloned.1.call-start = ((), (), s32[]{:S(2)}) async-start(), calls=%async_computation.5 | async-start | bytes 5242880 | tf_op jit(solution)/shard_map/all_gather | solution.py:72
  9.4 191.0 %all-gather.9.cloned.1.call-start = ((), (), s32[]{:S(2)}) async-start(), calls=%async_computation.4 | async-start | bytes 5242880 | tf_op jit(solution)/shard_map/all_gather | solution.py:84
  48.8 51.1 %copy-start.12 = (bf16[1,1,512,1024]{3,2,1,0:T(8,128)(2,1)S(1)}, bf16[1,1,512,1024]{3,2,1,0:T(8,128)(2,1)}, u32[]{:S(2)}) copy-start(bf16[1,1,512,1024]{3,2,1,0:T(8,128)(2,1)} %param.25) | copy-start | bytes 3145732
  48.8 301.2 %all-gather.15.cloned.1.call-start = ((), (), s32[]{:S(2)}) async-start(), calls=%async_computation.7 | async-start | bytes 10485760 | tf_op jit(solution)/shard_map/all_gather | solution.py:57
  48.9 47.6 %collective-permute-start = (bf16[1,1,512,2048]{3,2,1,0:T(8,128)(2,1)}, bf16[1,1,512,2048]{3,2,1,0:T(8,128)(2,1)S(1)}, u32[]{:S(2)}, u32[]{:S(2)}) collective-permute-start(bf16[1,1,512,2048]{3,2,1,0:T(8,128)(2,1)} %param.13), channel_id=1, source_target_pairs={{0,16},{16,0},{1,17},{17,1},{2,18},{18,2},{3,19},{19,3},{4,20},{20... | collective-permute-start | bytes 6291464 | tf_op jit(solution)/shard_map/ppermute | solution.py:13
  96.5 1.4 copy-start.11
  97.9 4.5 copy-start.17
  98.0 357.6 %all-gather.17.cloned.1.call-start = ((), (), s32[]{:S(2)}) async-start(), calls=%async_computation.8 | async-start | bytes 20971520 | tf_op jit(solution)/shard_map/all_gather | solution.py:64
  98.5 490.2 %reduce-scatter.4.cloned.1.call-start = ((), (), s32[]{:S(2)}) async-start(), calls=%async_computation.9 | async-start | bytes 5242880 | tf_op jit(solution)/shard_map/reduce_scatter | solution.py:109
  200.4 4.9 copy-start.14
  200.4 5.7 copy-start.5
  200.4 5.9 copy-start.10
  455.5 21.4 %copy-start.16 = (f32[1,8192]{1,0:T(1,128)S(1)}, f32[1,8192]{1,0:T(1,128)}, u32[]{:S(2)}) copy-start(f32[1,8192]{1,0:T(1,128)} %param.18) | copy-start | bytes 98308
  477.0 14.8 %copy-start.15 = (f32[1,128]{1,0:T(1,128)S(1)}, f32[1,128]{1,0:T(1,128)}, u32[]{:S(2)}) copy-start(f32[1,128]{1,0:T(1,128)} %param.22) | copy-start | bytes 1540
  498.1 3.9 copy-start.8
  498.1 4.7 copy-start.9
  498.1 4.7 copy-start.13
  498.1 4.7 copy-start.18
  502.0 2.3 copy-start.2
  504.0 2.2 copy-start.4
  506.2 2.2 copy-start.7
  511.8 151.9 %reduce-scatter.8.cloned.1.call-start = ((), (), s32[]{:S(2)}) async-start(), calls=%async_computation.11 | async-start | bytes 10485760 | tf_op jit(solution)/shard_map/reduce_scatter | solution.py:129
  511.9 5.5 copy-start.6
  528.3 170.1 %reduce-scatter.6.cloned.1.call-start = ((), (), s32[]{:S(2)}) async-start(), calls=%async_computation.10 | async-start | bytes 3145728 | tf_op jit(solution)/shard_map/reduce_scatter | solution.py:114
  595.5 3.7 copy-start.3
  600.3 98.1 %copy-start.1 = (s32[1,2]{1,0:T(1,128)S(1)}, s32[1,2]{1,0:T(1,128)}, u32[]{:S(2)}) copy-start(s32[1,2]{1,0:T(1,128)} %param.17) | copy-start | bytes 28
Sparse Core Ops, SparseCore 0:
  9.6 35.7 all-gather.6
  47.0 34.4 all-gather.12
  83.1 34.4 all-gather.10
  119.6 80.7 all-gather.8
  201.8 148.1 all-gather.14
  351.4 104.1 all-gather.16
  511.9 76.7 reduce-scatter.3
  591.5 72.2 reduce-scatter.7
  666.6 31.8 reduce-scatter.5
where the time goes:
time: 706 us; the launch traced here: 705 us
  waiting for transfers between devices  561 us (79%)
  local copies, waits for them, and re-layouts  51.3 us (7%)
  matrix products  44.1 us (6%)
  other arithmetic  30.3 us (4%)
  between operations  17.4 us (2%)
    all_gather x1, waiting for transfers between devices, per_device(): full_text = lax.all_gather(arrived, 'mp', axis=3, tiled=True)[0, 0]  140 us
    all_gather x1, waiting for transfers between devices, per_device(): lax.all_gather(query_weight, 'dp', axis=1, tiled=True)[0]  100 us
    all_gather x1, waiting for transfers between devices, per_device(): image = lax.all_gather(image_part, 'mp', axis=1, tiled=True)  76.4 us
    reduce_scatter x1, waiting for transfers between devices, per_device(): lax.psum_scatter(jnp.concatenate([key_part, value_part], axis=1).astype(j...  62.2 us
    reduce_scatter x1, waiting for transfers between devices, per_device(): lax.psum_scatter(partial_bf.astype(jnp.float32).astype(jnp.bfloat16), 'mp...  59.6 us
    ppermute x1, waiting for transfers between devices, shifted(): return lax.ppermute(value, axis, pairs)  47.3 us
    all_gather x1, waiting for transfers between devices, per_device(): shard_piece = lax.all_gather(vision, 'section', axis=1, tiled=True)  34.7 us
    reduce_scatter x1, waiting for transfers between devices, per_device(): lax.psum_scatter(jnp.where((row_ids // slot_rows == wanted)[:, None], tak...  30.4 us
  transfers between devices with their start and end apart: 10, of which 9 were waited for; matrix products, arithmetic and copies ran while one was open for 10% of the time, Pallas kernels for 0%

commit v1 on v0

--- a/solution.py
+++ b/solution.py
@@ -81,7 +81,12 @@
     chosen = (owners == wanted)[:, None, None]
     taken = jnp.where(chosen, shard_piece[0], jnp.zeros_like(shard_piece[0]))
     image_part = jnp.sum(taken.astype(jnp.float32), axis=0).astype(jnp.bfloat16)
-    image = lax.all_gather(image_part, "mp", axis=1, tiled=True)
+    ring = [image_part]
+    for hop in range(3):
+        ring.append(lax.ppermute(ring[-1], "mp", [(dev, (dev + 1) % 4) for dev in range(4)]))
+    image = jnp.roll(
+        jnp.concatenate(ring[::-1], axis=1), (lax.axis_index("mp") + 1) * ring[0].shape[1], axis=1
+    )
     width_k = key_full.shape[1]
     keys_raw = jnp.dot(image, key_full, preferred_element_type=jnp.float32).reshape(
         slot_rows, width_k // HD, HD

time: 706 us -> 656 us (0.929)
  waiting for transfers between devices: 561 us -> 485 us
  local copies, waits for them, and re-layouts: 51.3 us -> 66.2 us
    ppermute x0 -> x3, waiting for transfers between devices: none -> 79 us  [per_device(): lax.ppermute(ring[-1], 'mp', [(dev, (dev + 1) % 4) for dev in range(4)])]
    all_gather x1 -> x0, waiting for transfers between devices: 76.4 us -> none  [per_device(): image = lax.all_gather(image_part, 'mp', axis=1, tiled=True)]
    all_gather x1, waiting for transfers between devices: 140 us -> 85.6 us  [per_device(): full_text = lax.all_gather(arrived, 'mp', axis=3, tiled=True)[0, 0]]
    all_gather x1, waiting for transfers between devices: 34.7 us -> 0.02 us  [per_device(): shard_piece = lax.all_gather(vision, 'section', axis=1, tiled=True)]
    ppermute x1, waiting for transfers between devices: 47.3 us -> 68.3 us  [shifted(): return lax.ppermute(value, axis, pairs)]
    unnamed x40 -> x43, local copies, waits for them, and re-layouts: 6.98 us -> 19.9 us
  transfers between devices with their start and end apart: 10 -> 12, of which waited for: 9 -> 9; matrix products, arithmetic and copies ran while one was open for 10% -> 13% of each run, Pallas kernels for 0% -> 0%
where the time goes in v1:
time: 656 us; the launch traced here: 654 us
  waiting for transfers between devices  485 us (74%)
  local copies, waits for them, and re-layouts  66.2 us (10%)
  matrix products  50.2 us (8%)
  other arithmetic  29.4 us (4%)
  between operations  17.8 us (3%)
    all_gather x1, waiting for transfers between devices, per_device(): lax.all_gather(query_weight, 'dp', axis=1, tiled=True)[0]  100 us
    all_gather x1, waiting for transfers between devices, per_device(): full_text = lax.all_gather(arrived, 'mp', axis=3, tiled=True)[0, 0]  85.6 us
    ppermute x3, waiting for transfers between devices, per_device(): lax.ppermute(ring[-1], 'mp', [(dev, (dev + 1) % 4) for dev in range(4)])  79 us
    ppermute x1, waiting for transfers between devices, shifted(): return lax.ppermute(value, axis, pairs)  68.3 us
    reduce_scatter x1, waiting for transfers between devices, per_device(): lax.psum_scatter(jnp.concatenate([key_part, value_part], axis=1).astype(j...  62.2 us
    reduce_scatter x1, waiting for transfers between devices, per_device(): lax.psum_scatter(partial_bf.astype(jnp.float32).astype(jnp.bfloat16), 'mp...  57 us
    reduce_scatter x1, waiting for transfers between devices, per_device(): lax.psum_scatter(jnp.where((row_ids // slot_rows == wanted)[:, None], tak...  30.4 us
    dot_general x1, local copies, waits for them, and re-layouts, per_device(): jnp.dot(columns, lax.all_gather(query_weight, 'dp', axis=1, tiled=True)[0...  21.4 us
  transfers between devices with their start and end apart: 12, of which 9 were waited for; matrix products, arithmetic and copies ran while one was open for 13% of the time, Pallas kernels for 0%

profile of v1, /device:TPU:0, one launch (start us, length us, event | category | flops | bytes accessed | tf_op | source)
XLA Modules:
  0.0 654.3 jit_solution(2992196396561804734)
XLA Ops:
  7.2 0.7 all-gather.6.cloned.1.call-update
  8.0 0.7 all-gather.10.cloned.1.call-update
  8.7 0.7 all-gather.8.cloned.1.call-update
  9.4 3.0 collective-permute-start.3
  12.4 68.3 %collective-permute-done.3 = bf16[1,1,512,2048]{3,2,1,0:T(8,128)(2,1)S(1)} collective-permute-done((bf16[1,1,512,2048]{3,2,1,0:T(8,128)(2,1)}, bf16[1,1,512,2048]{3,2,1,0:T(8,128)(2,1)S(1)}, u32[]{:S(2)}, u32[]{:S(2)}) %collective-permute-start.3) | collective-permute-done | bytes 2097184 | tf_op jit(solution)/shard_map/ppermute | solution.py:13
  80.8 1.3 copy-done.10
  82.2 0.5 all-gather.14.cloned.1.call-update
  82.8 0.6 constant_dynamic-slice_fusion.1
  83.4 0.6 iota_compare_fusion.2
  84.1 2.5 fusion.38
  86.5 1.9 collective-permute-start
  88.4 24.3 %collective-permute-done = bf16[256,2048]{1,0:T(8,128)(2,1)S(1)} collective-permute-done((bf16[256,2048]{1,0:T(8,128)(2,1)S(1)}, bf16[256,2048]{1,0:T(8,128)(2,1)S(1)}, u32[]{:S(2)}, u32[]{:S(2)}) %collective-permute-start) | collective-permute-done | bytes 1048608 | tf_op jit(solution)/shard_map/ppermute | solution.py:86
  112.7 1.0 copy-done.8
  113.7 25.3 %collective-permute-done.1 = bf16[256,2048]{1,0:T(8,128)(2,1)} collective-permute-done((bf16[256,2048]{1,0:T(8,128)(2,1)S(1)}, bf16[256,2048]{1,0:T(8,128)(2,1)}, u32[]{:S(2)}, u32[]{:S(2)}) %collective-permute-start.1) | collective-permute-done | bytes 1048608 | tf_op jit(solution)/shard_map/ppermute | solution.py:86
  140.3 1.5 copy.81
  143.8 0.6 fusion.108
  144.4 1.2 iota_compare_fusion.1
  145.7 29.4 %collective-permute-done.2 = bf16[256,2048]{1,0:T(8,128)(2,1)} collective-permute-done((bf16[256,2048]{1,0:T(8,128)(2,1)}, bf16[256,2048]{1,0:T(8,128)(2,1)}, u32[]{:S(2)}, u32[]{:S(2)}) %collective-permute-start.2) | collective-permute-done | bytes 1048608 | tf_op jit(solution)/shard_map/ppermute | solution.py:86
  175.0 2.3 constant_dynamic-update-slice_fusion.7
  177.4 2.3 constant_dynamic-update-slice_fusion.6
  179.6 1.0 constant_dynamic-update-slice_fusion.5
  180.7 1.0 constant_dynamic-update-slice_fusion.4
  181.7 2.3 constant_dynamic-update-slice_fusion.3
  184.0 2.3 constant_dynamic-update-slice_fusion.2
  186.3 1.0 constant_dynamic-update-slice_fusion.1
  187.3 1.0 constant_dynamic-update-slice_fusion
  188.3 6.4 copy.51
  194.7 4.8 multiply_reduce_fusion.2
  199.5 0.7 multiply_convert_fusion.1
  200.3 6.4 copy.50
  206.7 4.7 fusion.64
  211.4 2.1 fusion.47
  213.6 85.6 %all-gather.12.cloned.1.call-done = bf16[1,1,512,8192]{3,2,1,0:T(8,128)(2,1)} async-done(((bf16[1,1,512,2048]{3,2,1,0:T(8,128)(2,1)}), bf16[1,1,512,8192]{3,2,1,0:T(8,128)(2,1)}) %all-gather.12.cloned.1.call-update) | async-done | bytes 8388624 | tf_op jit(solution)/shard_map/all_gather | solution.py:57
  299.1 5.1 fusion.1
  304.2 100.4 %all-gather.14.cloned.1.call-done = bf16[1,8192,1024]{2,1,0:T(8,128)(2,1)} async-done(((bf16[1,2048,1024]{2,1,0:T(8,128)(2,1)}), bf16[1,8192,1024]{2,1,0:T(8,128)(2,1)}) %all-gather.14.cloned.1.call-update) | async-done | bytes 16777232 | tf_op jit(solution)/shard_map/all_gather | solution.py:64
  404.6 21.4 %copy.52 = bf16[1024,8192]{1,0:T(8,128)(2,1)} copy(bf16[1024,8192]{0,1:T(8,128)(2,1)} %bitcast.148) | data formatting | bytes 33554432 | tf_op jit(solution)/shard_map/dot_general | solution.py:62
  426.0 14.8 %multiply_reduce_fusion = (f32[512,8]{0,1:T(8,128)S(1)}, f32[512,8,128]{0,2,1:T(8,128)S(1)}) fusion(bf16[8,128,8192]{2,1,0:T(8,128)(2,1)} %bitcast.149, bf16[1,1,512,8192]{3,2,1,0:T(8,128)(2,1)} %all-gather.12.cloned.1.call-done, f32[8192]{0:T(1024)S(1)} %bitcast.167, f32[512]{0:T(512)S(1)} %add_rsqrt_fusion.1), kind=kOutput, calls=%fused_computation.59 | convolution fusion | flops 8607756288 | bytes 27314176 | tf_op jit(solution)/shard_map/dot_general | solution.py:62
  440.8 0.5 multiply_convert_fusion
  441.3 5.1 fusion.109
  446.4 0.7 multiply_divide_fusion
  447.2 3.9 fusion.16
  451.1 0.7 copy-done.7
  451.8 1.2 fusion.70
  453.2 0.1 fusion.79
  453.4 0.8 fusion.67
  454.2 1.1 copy-done.4
  455.3 1.3 fusion.19
  456.6 0.9 copy-done.5
  457.4 3.4 fusion.4
  460.9 5.4 convolution_convert_fusion
  466.3 6.0 convolution_convert_fusion.1
  472.4 7.7 %pad_maximum_fusion = bf16[8192,512]{0,1:T(8,128)(2,1)} fusion(bf16[8192,256]{0,1:T(8,128)(2,1)} %convolution_convert_fusion, bf16[8192,256]{0,1:T(8,128)(2,1)} %convolution_convert_fusion.1), kind=kLoop, calls=%fused_computation.13 | loop fusion | flops 16777216 | bytes 16777216 | tf_op jit(solution)/shard_map/concatenate | solution.py:135
  480.1 0.7 fusion.93
  480.8 57.0 %reduce-scatter.4.cloned.1.call-done = bf16[256,2048]{1,0:T(8,128)(2,1)} async-done(((bf16[256,8192]{1,0:T(8,128)(2,1)}), bf16[256,2048]{1,0:T(8,128)(2,1)}) %reduce-scatter.4.cloned.1.call-update) | async-done | bytes 1048592 | tf_op jit(solution)/shard_map/reduce_scatter | solution.py:114
  537.8 6.8 %gather_fusion = bf16[512,2048]{1,0:T(8,128)(2,1)} fusion(bf16[256,2048]{1,0:T(8,128)(2,1)} %reduce-scatter.4.cloned.1.call-done, s32[1024]{0:T(1024)S(1)} %pad_clamp_fusion), kind=kCustom, calls=%fused_computation | custom fusion | bytes 4196352 | tf_op jit(solution)/shard_map/jit(_take)/gather | solution.py:118
  544.6 3.7 select_convert_fusion
  548.3 0.5 convolution_multiply_fusion
  548.8 0.5 copy.57
  549.4 1.2 select_convert_fusion.1
  550.6 62.2 %reduce-scatter.8.cloned.1.call-done = bf16[2048,512]{0,1:T(8,128)(2,1)} async-done(((bf16[8192,512]{0,1:T(8,128)(2,1)}), bf16[2048,512]{0,1:T(8,128)(2,1)}) %reduce-scatter.8.cloned.1.call-update) | async-done | bytes 2097168 | tf_op jit(solution)/shard_map/reduce_scatter | solution.py:134
  612.8 1.7 slice_bitcast_fusion
  614.5 1.3 copy.64
  615.8 1.3 copy.65
  617.1 30.4 %reduce-scatter.6.cloned.1.call-done = bf16[256,2048]{1,0:T(8,128)(2,1)} async-done(((bf16[512,2048]{1,0:T(8,128)(2,1)}), bf16[256,2048]{1,0:T(8,128)(2,1)}) %reduce-scatter.6.cloned.1.call-update) | async-done | bytes 1048592 | tf_op jit(solution)/shard_map/reduce_scatter | solution.py:119
  (56 shorter events, 0.7 us)
Async XLA Ops:
  7.2 75.6 %copy-start = (s32[1,2]{1,0:T(1,128)S(1)}, s32[1,2]{1,0:T(1,128)}, u32[]{:S(2)}) copy-start(s32[1,2]{1,0:T(1,128)} %param.17) | copy-start | bytes 28
  7.2 76.9 %all-gather.6.cloned.1.call-start = ((), (), s32[]{:S(2)}) async-start(), calls=%async_computation.3 | async-start | bytes 3145728 | tf_op jit(solution)/shard_map/all_gather | solution.py:79
  7.9 180.4 %all-gather.10.cloned.1.call-start = ((), (), s32[]{:S(2)}) async-start(), calls=%async_computation.5 | async-start | bytes 5242880 | tf_op jit(solution)/shard_map/all_gather | solution.py:71
  8.7 191.6 %all-gather.8.cloned.1.call-start = ((), (), s32[]{:S(2)}) async-start(), calls=%async_computation.4 | async-start | bytes 5242880 | tf_op jit(solution)/shard_map/all_gather | solution.py:72
  9.4 289.7 %all-gather.12.cloned.1.call-start = ((), (), s32[]{:S(2)}) async-start(), calls=%async_computation.6 | async-start | bytes 10485760 | tf_op jit(solution)/shard_map/all_gather | solution.py:57
  9.4 71.3 %collective-permute-start.3 = (bf16[1,1,512,2048]{3,2,1,0:T(8,128)(2,1)}, bf16[1,1,512,2048]{3,2,1,0:T(8,128)(2,1)S(1)}, u32[]{:S(2)}, u32[]{:S(2)}) collective-permute-start(bf16[1,1,512,2048]{3,2,1,0:T(8,128)(2,1)} %param.13), channel_id=1, source_target_pairs={{0,16},{16,0},{1,17},{17,1},{2,18},{18,2},{3,19},{19,3},{4,20},{20... | collective-permute-start | bytes 6291464 | tf_op jit(solution)/shard_map/ppermute | solution.py:13
  80.8 1.3 copy-start.10
  82.1 322.5 %all-gather.14.cloned.1.call-start = ((), (), s32[]{:S(2)}) async-start(), calls=%async_computation.7 | async-start | bytes 20971520 | tf_op jit(solution)/shard_map/all_gather | solution.py:64
  82.7 61.1 %copy-start.15 = (s32[1,2]{1,0:T(1,128)S(1)}, s32[1,2]{1,0:T(1,128)}, u32[]{:S(2)}) copy-start(s32[1,2]{1,0:T(1,128)} %param.15) | copy-start | bytes 28
  82.7 455.1 %reduce-scatter.4.cloned.1.call-start = ((), (), s32[]{:S(2)}) async-start(), calls=%async_computation.8 | async-start | bytes 5242880 | tf_op jit(solution)/shard_map/reduce_scatter | solution.py:114
  86.5 26.2 %collective-permute-start = (bf16[256,2048]{1,0:T(8,128)(2,1)S(1)}, bf16[256,2048]{1,0:T(8,128)(2,1)S(1)}, u32[]{:S(2)}, u32[]{:S(2)}) collective-permute-start(bf16[256,2048]{1,0:T(8,128)(2,1)S(1)} %fusion.38), channel_id=1, source_target_pairs={{0,4},{4,8},{8,12},{12,0},{1,5},{5,9},{9,13},{13,1},{2,6},{6,10},{... | collective-permute-start | bytes 3145736 | tf_op jit(solution)/shard_map/ppermute | solution.py:86
  112.7 1.0 copy-start.8
  113.7 25.3 %collective-permute-start.1 = (bf16[256,2048]{1,0:T(8,128)(2,1)S(1)}, bf16[256,2048]{1,0:T(8,128)(2,1)}, u32[]{:S(2)}, u32[]{:S(2)}) collective-permute-start(bf16[256,2048]{1,0:T(8,128)(2,1)S(1)} %collective-permute-done), channel_id=1, source_target_pairs={{0,4},{4,8},{8,12},{12,0},{1,5},{5,9},{9,13},{13,1},{2,6},{6,10},{... | collective-permute-start | bytes 3145736 | tf_op jit(solution)/shard_map/ppermute | solution.py:86
  139.0 36.0 %collective-permute-start.2 = (bf16[256,2048]{1,0:T(8,128)(2,1)}, bf16[256,2048]{1,0:T(8,128)(2,1)}, u32[]{:S(2)}, u32[]{:S(2)}) collective-permute-start(bf16[256,2048]{1,0:T(8,128)(2,1)} %collective-permute-done.1), channel_id=1, source_target_pairs={{0,4},{4,8},{8,12},{12,0},{1,5},{5,9},{9,13},{13,1},{2,6},{6,10},{... | collective-permute-start | bytes 3145736 | tf_op jit(solution)/shard_map/ppermute | solution.py:86
  144.4 35.2 %copy-start.9 = (bf16[256,2048]{1,0:T(8,128)(2,1)S(1)}, bf16[256,2048]{1,0:T(8,128)(2,1)}, u32[]{:S(2)}) copy-start(bf16[256,2048]{1,0:T(8,128)(2,1)} %copy-done.8) | copy-start | bytes 3145732
  194.7 4.8 copy-start.12
  404.6 21.4 %copy-start.14 = (f32[1,8192]{1,0:T(1,128)S(1)}, f32[1,8192]{1,0:T(1,128)}, u32[]{:S(2)}) copy-start(f32[1,8192]{1,0:T(1,128)} %param.18) | copy-start | bytes 98308
  426.0 14.8 %copy-start.13 = (f32[1,128]{1,0:T(1,128)S(1)}, f32[1,128]{1,0:T(1,128)}, u32[]{:S(2)}) copy-start(f32[1,128]{1,0:T(1,128)} %param.22) | copy-start | bytes 1540
  447.2 3.9 copy-start.6
  447.2 4.7 copy-start.7
  447.2 4.7 copy-start.11
  447.2 4.7 copy-start.16
  451.1 2.3 copy-start.2
  453.1 2.2 copy-start.4
  455.3 2.2 copy-start.5
  460.9 151.9 %reduce-scatter.8.cloned.1.call-start = ((), (), s32[]{:S(2)}) async-start(), calls=%async_computation.10 | async-start | bytes 10485760 | tf_op jit(solution)/shard_map/reduce_scatter | solution.py:134
  480.1 167.4 %reduce-scatter.6.cloned.1.call-start = ((), (), s32[]{:S(2)}) async-start(), calls=%async_computation.9 | async-start | bytes 3145728 | tf_op jit(solution)/shard_map/reduce_scatter | solution.py:119
  544.6 3.7 copy-start.3
  549.4 98.1 %copy-start.1 = (s32[1,2]{1,0:T(1,128)S(1)}, s32[1,2]{1,0:T(1,128)}, u32[]{:S(2)}) copy-start(s32[1,2]{1,0:T(1,128)} %param.17) | copy-start | bytes 28
Sparse Core Ops, SparseCore 0:
  9.6 58.3 all-gather.5
  69.6 34.4 all-gather.9
  105.6 34.4 all-gather.7
  141.6 157.4 all-gather.11
  300.5 104.0 all-gather.13
  461.0 76.7 reduce-scatter.3
  540.5 72.2 reduce-scatter.7
  615.6 31.8 reduce-scatter.5
